TPU v7x, 32 devices: a whole 2x2x4 slice. The times are simulated.
32 devices in a mesh: shard: 4 (over z), rep: 8 (over y, x, core).
Axes of the slice: x: 2, y: 2, z: 4, core: 2. Of those that a mesh axis runs over, the one named last changes fastest.
Arguments:
- grads: bfloat16 [1, 8192, 28672], P(None, 'shard', 'rep'), may hold values from -81 to 81
- seeds: int32 [1], replicated, may hold values from 0 to 999999
Outputs:
- projected: bfloat16 [512, 1, 28672], P('shard', None, 'rep')
All inputs are finite; a program needn't handle non-finite values.
Results may differ from a plain program's by a relative error of at most 0.0056.
Values may be sent and summed in bfloat16 or wider, within the bound.
No kernel may reach another device: no remote copies, remote signals or barrier semaphores. Data moves between devices by JAX's collectives and lax.ppermute only.
A program may use at most 128 MiB of HBM per device.

v0:
```python
import jax
import jax.numpy as jnp
from jax import lax
from jax.sharding import PartitionSpec as P

RANK = 512
mix_first = 668265263
mix_second = -2048144789
mix_third = -1028477387


def sketch_table(seeds, first_row, count, rank):
    rows = first_row + lax.iota(jnp.int32, count)
    columns = lax.iota(jnp.int32, rank)
    counter = rows[:, None] * jnp.int32(rank) + columns[None, :]
    hashed = jnp.bitwise_xor(counter[None, :, :], (seeds * jnp.int32(mix_first))[:, None, None])
    hashed = hashed * jnp.int32(mix_second)
    hashed = jnp.bitwise_xor(hashed, lax.shift_right_logical(hashed, jnp.int32(15)))
    hashed = hashed * jnp.int32(mix_third)
    hashed = jnp.bitwise_xor(hashed, lax.shift_right_logical(hashed, jnp.int32(13)))
    unit = lax.shift_right_logical(hashed, jnp.int32(8)).astype(jnp.float32) * (1.0 / 16777216.0)
    return (2.0 * unit - 1.0).astype(jnp.bfloat16)


def body(grads, seeds):
    mats, depth, width = grads.shape
    col0 = lax.axis_index("rep") * width
    outs = []
    for m in range(mats):
        table = sketch_table(seeds[m : m + 1], col0, width, RANK)[0]
        g = grads[m]
        partial = jnp.dot(g, table, preferred_element_type=jnp.float32)
        sketch_rows = lax.psum(partial, "rep")
        local_gram = jnp.dot(
            sketch_rows.T,
            sketch_rows,
            precision=lax.Precision.HIGHEST,
            preferred_element_type=jnp.float32,
        )
        piece = local_gram.shape[0] // lax.axis_size("rep")
        mine = lax.dynamic_slice_in_dim(local_gram, lax.axis_index("rep") * piece, piece, 0)
        gram = lax.all_gather(lax.psum(mine, "shard"), "rep", axis=0, tiled=True)
        factor = jnp.linalg.cholesky(gram)
        basis_rows = lax.linalg.triangular_solve(
            factor, sketch_rows, left_side=False, lower=True, transpose_a=True
        ).astype(jnp.bfloat16)
        partial_sum = jnp.dot(basis_rows.T, g, preferred_element_type=jnp.float32)
        outs.append(partial_sum)
    partial_sum = jnp.stack(outs, axis=1)
    projected = lax.psum_scatter(partial_sum, "shard", scatter_dimension=0, tiled=True)
    return projected.astype(jnp.bfloat16)


def solution(mesh):
    return jax.shard_map(
        body,
        mesh=mesh,
        in_specs=(P(None, "shard", "rep"), P()),
        out_specs=P("shard", None, "rep"),
        check_vma=False,
    )
```

profile of v0, /device:TPU:0, one launch (start us, length us, event | category | flops | bytes accessed | tf_op | source)
XLA Modules:
  0.0 482.1 jit_solution(17405715005233900256)
XLA Ops:
  7.2 16.7 %fusion.24 = f32[2048,512]{0,1:T(8,128)} fusion(bf16[1,2048,3584]{2,1,0:T(8,128)(2,1)} %param.2, s32[]{:T(128)} %bitcast, s32[3584]{0:T(1024)S(1)} %add_multiply_fusion), kind=kOutput, calls=%fused_computation.25 | convolution fusion | flops 7540047872 | bytes 18888708 | tf_op jit(solution)/shard_map/dot_general | solution.py:32
  24.3 83.4 %all-reduce.4.cloned.1.call-done = f32[2048,512]{0,1:T(8,128)} async-done(((f32[2048,512]{0,1:T(8,128)}), f32[2048,512]{0,1:T(8,128)}) %all-reduce.4.cloned.1.call-update) | async-done | bytes 4194320 | tf_op jit(solution)/shard_map/psum | solution.py:33
  107.6 9.3 %fusion.81 = f32[512,512]{1,0:T(8,128)S(1)} fusion(f32[2048,512]{0,1:T(8,128)} %all-reduce.4.cloned.1.call-done), kind=kOutput, calls=%fused_computation.111 | convolution fusion | flops 6442450944 | bytes 5242880 | tf_op jit(solution)/shard_map/dot_general | solution.py:34
  117.7 34.8 %all-reduce.6.cloned.1.call-done = f32[64,512]{1,0:T(8,128)} async-done(((f32[64,512]{1,0:T(8,128)}), f32[64,512]{1,0:T(8,128)}) %all-reduce.6.cloned.1.call-update) | async-done | bytes 131088 | tf_op jit(solution)/shard_map/psum | solution.py:42
  152.6 24.9 %all-gather.2.cloned.1.call-done = f32[512,512]{1,0:T(8,128)} async-done(((f32[64,512]{1,0:T(8,128)}), f32[512,512]{1,0:T(8,128)}) %all-gather.2.cloned.1.call-update) | async-done | bytes 1048592 | tf_op jit(solution)/shard_map/all_gather | solution.py:42
  177.5 1.6 copy.7
  179.1 1.4 fusion.50
  180.6 11.7 %cholesky.104 = f32[128,128]{1,0:T(8,128)S(1)} custom-call(f32[128,128]{1,0:T(8,128)S(1)} %cholesky.266), custom_call_target="Cholesky" | custom-call | tf_op jit(solution)/shard_map/jit(cholesky)/cholesky | solution.py:43
  192.3 9.8 %custom-call.30 = f32[1,128,128]{1,2,0:T(8,128)S(1)} custom-call(f32[1,128,128]{2,1,0:T(8,128)S(1)} %get-tuple-element.32), custom_call_target="InvertDiagBlocksLowerTriangular" | custom-call | tf_op jit(solution)/shard_map/jit(cholesky)/cholesky | solution.py:43
  202.9 11.7 %cholesky.217 = f32[128,128]{1,0:T(8,128)S(1)} custom-call(f32[128,128]{1,0:T(8,128)S(1)} %cholesky.270), custom_call_target="Cholesky" | custom-call | tf_op jit(solution)/shard_map/jit(cholesky)/cholesky | solution.py:43
  214.7 18.5 %custom-call.31 = f32[1,128,128]{1,2,0:T(8,128)S(1)} custom-call(f32[1,128,128]{2,1,0:T(8,128)S(1)} %get-tuple-element.29), custom_call_target="InvertDiagBlocksLowerTriangular" | custom-call | tf_op jit(solution)/shard_map/jit(cholesky)/cholesky | solution.py:43
  233.9 11.7 %cholesky.238 = f32[128,128]{1,0:T(8,128)S(1)} custom-call(f32[128,128]{1,0:T(8,128)S(1)} %cholesky.275), custom_call_target="Cholesky" | custom-call | tf_op jit(solution)/shard_map/jit(cholesky)/cholesky | solution.py:43
  246.3 9.8 %custom-call.32 = f32[1,128,128]{1,2,0:T(8,128)S(1)} custom-call(f32[1,128,128]{2,1,0:T(8,128)S(1)} %get-tuple-element.26), custom_call_target="InvertDiagBlocksLowerTriangular" | custom-call | tf_op jit(solution)/shard_map/jit(cholesky)/cholesky | solution.py:43
  256.7 11.7 %cholesky.255 = f32[128,128]{1,0:T(8,128)S(1)} custom-call(f32[128,128]{1,0:T(8,128)S(1)} %convolution_subtract_fusion.4), custom_call_target="Cholesky" | custom-call | tf_op jit(solution)/shard_map/jit(cholesky)/cholesky | solution.py:43
  272.7 7.9 %while.1 = (s32[]{:T(128)}, f32[512,512]{1,0:T(8,128)S(1)}, s32[4,2]{0,1:T(2,128)S(1)}, f32[4,128,128]{2,1,0:T(8,128)S(1)}, s32[]{:T(128)}) while((s32[]{:T(128)}, f32[512,512]{1,0:T(8,128)S(1)}, s32[4,2]{0,1:T(2,128)S(1)}, f32[4,128,128]{2,1,0:T(8,128)S(1)}, s32[]{:T(128)}) %tuple.30), condition=%wide.while_cond, body=%wide.while_body.sunk | while | flops 2 | bytes 131189 | solution.py:44
  273.4 1.4 bitcast_dynamic-update-slice_fusion.2
  275.3 1.4 bitcast_dynamic-update-slice_fusion.2
  280.7 39.3 %custom-call.33 = f32[4,128,128]{1,2,0:T(8,128)S(1)} custom-call(f32[4,128,128]{2,1,0:T(8,128)S(1)} %get-tuple-element.12), custom_call_target="InvertDiagBlocksLowerTriangular" | custom-call | tf_op jit(solution)/shard_map/triangular_solve | solution.py:44
  320.0 2.5 fusion.80
  322.4 2.3 convolution_subtract_fusion.1
  328.3 2.2 fusion.35
  331.6 13.1 %fusion.10 = f32[512,1,3584]{2,0,1:T(8,128)} fusion(bf16[1,2048,3584]{2,1,0:T(8,128)(2,1)} %param.2, bf16[2048,128]{0,1:T(8,128)(2,1)S(1)} %convolution_convert_fusion, bf16[2048,128]{0,1:T(8,128)(2,1)S(1)} %get-tuple-element.35, bf16[2048,128]{0,1:T(8,128)(2,1)S(1)} %get-tuple-element.37, bf16[2048,128]{0,1:T(8,128)(2,1)S(1)} %get-tuple-element.39), kind=kOutput, calls=%fused_computation.14 | convolution fusion | flops 7524581376 | bytes 24117248 | tf_op jit(solution)/shard_map/dot_general | solution.py:47
  344.7 127.9 %reduce-scatter.2.cloned.1.call-done = f32[128,1,3584]{2,0,1:T(8,128)} async-done(((f32[512,1,3584]{2,0,1:T(8,128)}), f32[128,1,3584]{2,0,1:T(8,128)}) %reduce-scatter.2.cloned.1.call-update) | async-done | bytes 1835024 | tf_op jit(solution)/shard_map/reduce_scatter | solution.py:50
  472.6 2.5 convert_element_type.47
  (47 shorter events, 15.3 us)
Async XLA Ops:
  6.5 101.1 %all-reduce.4.cloned.1.call-start = ((), (), s32[]{:S(2)}) async-start(), calls=%async_computation.1 | async-start | bytes 8388608 | tf_op jit(solution)/shard_map/psum | solution.py:33
  23.9 128.6 %all-reduce.6.cloned.1.call-start = ((), (), s32[]{:S(2)}) async-start(), calls=%async_computation.2 | async-start | bytes 262144 | tf_op jit(solution)/shard_map/psum | solution.py:42
  117.7 59.9 %all-gather.2.cloned.1.call-start = ((), (), s32[]{:S(2)}) async-start(), calls=%async_computation.3 | async-start | bytes 1179648 | tf_op jit(solution)/shard_map/all_gather | solution.py:42
  152.6 320.0 %reduce-scatter.2.cloned.1.call-start = ((), (), s32[]{:S(2)}) async-start(), calls=%async_computation.4 | async-start | bytes 9175040 | tf_op jit(solution)/shard_map/reduce_scatter | solution.py:50
  320.0 5.9 %copy-start = (f32[2048,512]{0,1:T(8,128)S(1)}, f32[2048,512]{0,1:T(8,128)}, u32[]{:S(2)}) copy-start(f32[2048,512]{0,1:T(8,128)} %all-reduce.4.cloned.1.call-done) | copy-start | bytes 12582916
Sparse Core Ops, SparseCore 0:
  24.1 83.5 all-reduce.3
  117.8 34.7 all-reduce.5
  154.5 23.0 all-gather.1
  344.8 127.7 reduce-scatter.1
where the time goes:
time: 490 us; the launch traced here: 482 us
  waiting for transfers between devices  271 us (55%)
  other arithmetic  131 us (27%)
  matrix products  52.5 us (11%)
  between operations  17 us (3%)
  local copies, waits for them, and re-layouts  10.2 us (2%)
    reduce_scatter x1, waiting for transfers between devices, body(): lax.psum_scatter(partial_sum, 'shard', scatter_dimension=0, tiled=True)  128 us
    another operation x14, other arithmetic, body(): factor = jnp.linalg.cholesky(gram)  87.2 us
    psum x1, waiting for transfers between devices, body(): sketch_rows = lax.psum(partial, 'rep')  83.4 us
    another operation x3, other arithmetic, body(): lax.linalg.triangular_solve(factor, sketch_rows, left_side=False, lower=T...  39.7 us
    psum x1, waiting for transfers between devices, body(): gram = lax.all_gather(lax.psum(mine, 'shard'), 'rep', axis=0, tiled=True)  34.8 us
    all_gather x1, waiting for transfers between devices, body(): gram = lax.all_gather(lax.psum(mine, 'shard'), 'rep', axis=0, tiled=True)  24.9 us
    dot_general x1, matrix products, body(): partial = jnp.dot(g, table, preferred_element_type=jnp.float32)  16.7 us
    dot_general x1, matrix products, body(): partial_sum = jnp.dot(basis_rows.T, g, preferred_element_type=jnp.float32)  13.1 us
  transfers between devices with their start and end apart: 4, of which 4 were waited for; matrix products, arithmetic and copies ran while one was open for 0% of the time, Pallas kernels for 0%

commit v1 on v0

--- a/solution.py
+++ b/solution.py
@@ -30,7 +30,11 @@
         table = sketch_table(seeds[m : m + 1], col0, width, RANK)[0]
         g = grads[m]
         partial = jnp.dot(g, table, preferred_element_type=jnp.float32)
-        sketch_rows = lax.psum(partial, "rep")
+        sketch_rows = partial
+        for hop in (1, 2, 4):
+            sketch_rows = sketch_rows + lax.ppermute(
+                sketch_rows, "rep", [(dev, dev ^ hop) for dev in range(8)]
+            )
         local_gram = jnp.dot(
             sketch_rows.T,
             sketch_rows,

time: 490 us -> 600 us (1.22)
  waiting for transfers between devices: 271 us -> 377 us
    ppermute x0 -> x3, waiting for transfers between devices: none -> 188 us  [body(): lax.ppermute(sketch_rows, 'rep', [(dev, dev ^ hop) for dev in range(8)])]
    psum x1 -> x0, waiting for transfers between devices: 83.4 us -> none  [body(): sketch_rows = lax.psum(partial, 'rep')]
    add x0 -> x3, other arithmetic: none -> 10.1 us  [body(): sketch_rows + lax.ppermute(sketch_rows, 'rep', [(dev, dev ^ hop) for dev...]
    another operation x14, other arithmetic: 87.2 us -> 78.6 us  [body(): factor = jnp.linalg.cholesky(gram)]
  transfers between devices with their start and end apart: 4 -> 6, of which waited for: 4 -> 6; matrix products, arithmetic and copies ran while one was open for 0% -> 0% of each run, Pallas kernels for 0% -> 0%
where the time goes in v1:
time: 600 us; the launch traced here: 591 us
  waiting for transfers between devices  377 us (63%)
  other arithmetic  132 us (22%)
  matrix products  49 us (8%)
  between operations  17 us (3%)
  local copies, waits for them, and re-layouts  10.2 us (2%)
    ppermute x3, waiting for transfers between devices, body(): lax.ppermute(sketch_rows, 'rep', [(dev, dev ^ hop) for dev in range(8)])  188 us
    reduce_scatter x1, waiting for transfers between devices, body(): lax.psum_scatter(partial_sum, 'shard', scatter_dimension=0, tiled=True)  128 us
    another operation x14, other arithmetic, body(): factor = jnp.linalg.cholesky(gram)  78.6 us
    another operation x3, other arithmetic, body(): lax.linalg.triangular_solve(factor, sketch_rows, left_side=False, lower=T...  39.7 us
    psum x1, waiting for transfers between devices, body(): gram = lax.all_gather(lax.psum(mine, 'shard'), 'rep', axis=0, tiled=True)  36 us
    all_gather x1, waiting for transfers between devices, body(): gram = lax.all_gather(lax.psum(mine, 'shard'), 'rep', axis=0, tiled=True)  24.5 us
    dot_general x1, matrix products, body(): partial = jnp.dot(g, table, preferred_element_type=jnp.float32)  16.7 us
    dot_general x1, matrix products, body(): partial_sum = jnp.dot(basis_rows.T, g, preferred_element_type=jnp.float32)  13.1 us
  transfers between devices with their start and end apart: 6, of which 6 were waited for; matrix products, arithmetic and copies ran while one was open for 0% of the time, Pallas kernels for 0%

profile of v1, /device:TPU:0, one launch (start us, length us, event | category | flops | bytes accessed | tf_op | source)
XLA Modules:
  0.0 591.1 jit_solution(12333221803121521751)
XLA Ops:
  7.2 16.7 %fusion.24 = f32[2048,512]{0,1:T(8,128)} fusion(bf16[1,2048,3584]{2,1,0:T(8,128)(2,1)} %param.2, s32[]{:T(128)} %bitcast, s32[3584]{0:T(1024)S(1)} %add_multiply_fusion), kind=kOutput, calls=%fused_computation.25 | convolution fusion | flops 7540047872 | bytes 18888708 | tf_op jit(solution)/shard_map/dot_general | solution.py:32
  24.4 7.0 %collective-permute-done = f32[2048,512]{0,1:T(8,128)S(1)} collective-permute-done((f32[2048,512]{0,1:T(8,128)}, f32[2048,512]{0,1:T(8,128)S(1)}, u32[]{:S(2)}, u32[]{:S(2)}) %collective-permute-start) | collective-permute-done | bytes 4194336 | tf_op jit(solution)/shard_map/ppermute | solution.py:35
  31.4 2.9 add.116
  34.3 2.9 collective-permute-start.1
  37.2 90.9 %collective-permute-done.1 = f32[2048,512]{0,1:T(8,128)S(1)} collective-permute-done((f32[2048,512]{0,1:T(8,128)S(1)}, f32[2048,512]{0,1:T(8,128)S(1)}, u32[]{:S(2)}, u32[]{:S(2)}) %collective-permute-start.1) | collective-permute-done | bytes 4194336 | tf_op jit(solution)/shard_map/ppermute | solution.py:35
  128.1 2.7 add.117
  132.6 90.6 %collective-permute-done.2 = f32[2048,512]{0,1:T(8,128)} collective-permute-done((f32[2048,512]{0,1:T(8,128)}, f32[2048,512]{0,1:T(8,128)}, u32[]{:S(2)}, u32[]{:S(2)}) %collective-permute-start.2) | collective-permute-done | bytes 4194336 | tf_op jit(solution)/shard_map/ppermute | solution.py:35
  223.1 4.4 add.118
  227.6 6.9 %fusion.80 = f32[512,512]{1,0:T(8,128)S(1)} fusion(f32[2048,512]{0,1:T(8,128)S(1)} %add.118), kind=kOutput, calls=%fused_computation.113 | convolution fusion | flops 6442450944 | bytes 5242880 | tf_op jit(solution)/shard_map/dot_general | solution.py:38
  235.3 36.0 %all-reduce.3.cloned.1.call-done = f32[64,512]{1,0:T(8,128)} async-done(((f32[64,512]{1,0:T(8,128)}), f32[64,512]{1,0:T(8,128)}) %all-reduce.3.cloned.1.call-update) | async-done | bytes 131088 | tf_op jit(solution)/shard_map/psum | solution.py:46
  271.7 24.5 %all-gather.2.cloned.1.call-done = f32[512,512]{1,0:T(8,128)} async-done(((f32[64,512]{1,0:T(8,128)}), f32[512,512]{1,0:T(8,128)}) %all-gather.2.cloned.1.call-update) | async-done | bytes 1048592 | tf_op jit(solution)/shard_map/all_gather | solution.py:46
  299.2 11.7 %cholesky.104 = f32[128,128]{1,0:T(8,128)S(1)} custom-call(f32[128,128]{1,0:T(8,128)S(1)} %cholesky.266), custom_call_target="Cholesky" | custom-call | tf_op jit(solution)/shard_map/jit(cholesky)/cholesky | solution.py:47
  311.0 9.8 %custom-call.30 = f32[1,128,128]{1,2,0:T(8,128)S(1)} custom-call(f32[1,128,128]{2,1,0:T(8,128)S(1)} %get-tuple-element.32), custom_call_target="InvertDiagBlocksLowerTriangular" | custom-call | tf_op jit(solution)/shard_map/jit(cholesky)/cholesky | solution.py:47
  321.6 11.7 %cholesky.217 = f32[128,128]{1,0:T(8,128)S(1)} custom-call(f32[128,128]{1,0:T(8,128)S(1)} %cholesky.270), custom_call_target="Cholesky" | custom-call | tf_op jit(solution)/shard_map/jit(cholesky)/cholesky | solution.py:47
  333.4 10.0 %custom-call.31 = f32[1,128,128]{1,2,0:T(8,128)S(1)} custom-call(f32[1,128,128]{2,1,0:T(8,128)S(1)} %get-tuple-element.29), custom_call_target="InvertDiagBlocksLowerTriangular" | custom-call | tf_op jit(solution)/shard_map/jit(cholesky)/cholesky | solution.py:47
  344.0 11.7 %cholesky.238 = f32[128,128]{1,0:T(8,128)S(1)} custom-call(f32[128,128]{1,0:T(8,128)S(1)} %cholesky.275), custom_call_target="Cholesky" | custom-call | tf_op jit(solution)/shard_map/jit(cholesky)/cholesky | solution.py:47
  356.4 9.8 %custom-call.32 = f32[1,128,128]{1,2,0:T(8,128)S(1)} custom-call(f32[1,128,128]{2,1,0:T(8,128)S(1)} %get-tuple-element.26), custom_call_target="InvertDiagBlocksLowerTriangular" | custom-call | tf_op jit(solution)/shard_map/jit(cholesky)/cholesky | solution.py:47
  366.8 11.7 %cholesky.255 = f32[128,128]{1,0:T(8,128)S(1)} custom-call(f32[128,128]{1,0:T(8,128)S(1)} %convolution_subtract_fusion.2), custom_call_target="Cholesky" | custom-call | tf_op jit(solution)/shard_map/jit(cholesky)/cholesky | solution.py:47
  382.9 7.9 %while.1 = (s32[]{:T(128)}, f32[512,512]{1,0:T(8,128)S(1)}, s32[4,2]{0,1:T(2,128)S(1)}, f32[4,128,128]{2,1,0:T(8,128)S(1)}, s32[]{:T(128)}) while((s32[]{:T(128)}, f32[512,512]{1,0:T(8,128)S(1)}, s32[4,2]{0,1:T(2,128)S(1)}, f32[4,128,128]{2,1,0:T(8,128)S(1)}, s32[]{:T(128)}) %tuple.30), condition=%wide.while_cond, body=%wide.while_body.sunk | while | flops 2 | bytes 131189 | solution.py:48
  390.8 39.3 %custom-call.33 = f32[4,128,128]{1,2,0:T(8,128)S(1)} custom-call(f32[4,128,128]{2,1,0:T(8,128)S(1)} %get-tuple-element.12), custom_call_target="InvertDiagBlocksLowerTriangular" | custom-call | tf_op jit(solution)/shard_map/triangular_solve | solution.py:48
  430.1 2.5 fusion.79
  440.6 13.1 %fusion.10 = f32[512,1,3584]{2,0,1:T(8,128)} fusion(bf16[1,2048,3584]{2,1,0:T(8,128)(2,1)} %param.2, bf16[2048,128]{0,1:T(8,128)(2,1)S(1)} %convolution_convert_fusion, bf16[2048,128]{0,1:T(8,128)(2,1)S(1)} %get-tuple-element.35, bf16[2048,128]{0,1:T(8,128)(2,1)S(1)} %get-tuple-element.37, bf16[2048,128]{0,1:T(8,128)(2,1)S(1)} %get-tuple-element.39), kind=kOutput, calls=%fused_computation.14 | convolution fusion | flops 7524581376 | bytes 24117248 | tf_op jit(solution)/shard_map/dot_general | solution.py:51
  453.7 127.9 %reduce-scatter.2.cloned.1.call-done = f32[128,1,3584]{2,0,1:T(8,128)} async-done(((f32[512,1,3584]{2,0,1:T(8,128)}), f32[128,1,3584]{2,0,1:T(8,128)}) %reduce-scatter.2.cloned.1.call-update) | async-done | bytes 1835024 | tf_op jit(solution)/shard_map/reduce_scatter | solution.py:54
  581.6 2.5 convert_element_type.47
  (55 shorter events, 26.8 us)
Async XLA Ops:
  6.5 264.7 %all-reduce.3.cloned.1.call-start = ((), (), s32[]{:S(2)}) async-start(), calls=%async_computation.1 | async-start | bytes 262144 | tf_op jit(solution)/shard_map/psum | solution.py:46
  23.9 7.5 %collective-permute-start = (f32[2048,512]{0,1:T(8,128)}, f32[2048,512]{0,1:T(8,128)S(1)}, u32[]{:S(2)}, u32[]{:S(2)}) collective-permute-start(f32[2048,512]{0,1:T(8,128)} %fusion.24), channel_id=1, source_target_pairs={{0,1},{1,0},{2,3},{3,2},{4,5},{5,4},{6,7},{7,6},{8,9},{9,8},{10,11... | collective-permute-start | bytes 12582920 | tf_op jit(solution)/shard_map/ppermute | solution.py:35
  34.3 93.8 %collective-permute-start.1 = (f32[2048,512]{0,1:T(8,128)S(1)}, f32[2048,512]{0,1:T(8,128)S(1)}, u32[]{:S(2)}, u32[]{:S(2)}) collective-permute-start(f32[2048,512]{0,1:T(8,128)S(1)} %add.116), channel_id=1, source_target_pairs={{0,2},{1,3},{2,0},{3,1},{4,6},{5,7},{6,4},{7,5},{8,10},{9,11},{10,... | collective-permute-start | bytes 12582920 | tf_op jit(solution)/shard_map/ppermute | solution.py:35
  130.8 92.4 %collective-permute-start.2 = (f32[2048,512]{0,1:T(8,128)}, f32[2048,512]{0,1:T(8,128)}, u32[]{:S(2)}, u32[]{:S(2)}) collective-permute-start(f32[2048,512]{0,1:T(8,128)} %add.117), channel_id=1, source_target_pairs={{0,4},{1,5},{2,6},{3,7},{4,0},{5,1},{6,2},{7,3},{8,12},{9,13},{10,... | collective-permute-start | bytes 12582920 | tf_op jit(solution)/shard_map/ppermute | solution.py:35
  227.6 6.9 %copy-start = (f32[2048,512]{0,1:T(8,128)}, f32[2048,512]{0,1:T(8,128)S(1)}, u32[]{:S(2)}) copy-start(f32[2048,512]{0,1:T(8,128)S(1)} %add.118) | copy-start | bytes 12582916
  235.2 61.0 %all-gather.2.cloned.1.call-start = ((), (), s32[]{:S(2)}) async-start(), calls=%async_computation.2 | async-start | bytes 1179648 | tf_op jit(solution)/shard_map/all_gather | solution.py:46
  271.3 310.4 %reduce-scatter.2.cloned.1.call-start = ((), (), s32[]{:S(2)}) async-start(), calls=%async_computation.3 | async-start | bytes 9175040 | tf_op jit(solution)/shard_map/reduce_scatter | solution.py:54
  430.1 3.5 copy-start.1
Sparse Core Ops, SparseCore 0:
  235.3 35.8 all-reduce.2
  273.1 23.0 all-gather.1
  453.8 127.7 reduce-scatter.1
